TPU v7x, 512 devices: a whole 4x4x16 slice. The times are simulated.
512 devices in a mesh: dp: 64 (over y, z), tensor: 8 (over x, core).
Axes of the slice: x: 4, y: 4, z: 16, core: 2. Of those that a mesh axis runs over, the one named last changes fastest.
Arguments:
- tokens: bfloat16 [65536, 1408], P(('dp', 'tensor')), may hold values from -6 to 6
- ln1_gain: float32 [1408], replicated, may hold values from 0.1 to 1.9
- ln1_shift: float32 [1408], replicated, may hold values from -3 to 3
- w_qkv: bfloat16 [1408, 16, 264], P(None, 'tensor')
- w_out: bfloat16 [16, 88, 1408], P('tensor'), may hold values from -0.625 to 0.625
- ln2_gain: float32 [1408], replicated, may hold values from 0.1 to 1.9
- ln2_shift: float32 [1408], replicated, may hold values from -3 to 3
- w_proj: bfloat16 [5632, 3584], P('dp', 'tensor'), may hold values from -0.078125 to 0.078125
- proj_bias: float32 [3584], P('tensor'), may hold values from -3 to 3
- segments: int32 [64, 256], P('dp'), may hold values from 0 to 7, never falling along the last dimension, each value on 1 to 128 neighbouring positions
- owners: int32 [16384, 1], P('dp'), may hold values from 0 to 63; in each aligned block of 256 rows (0 to 255, 256 to 511, ...) at most 8 rows name the same one
Outputs:
- delivered: bfloat16 [32768, 3584], P('dp', 'tensor')
Inputs may be any that keep to these rules, and one draw needn't show every extreme that they name: `segments`: within a pack numbers never fall, every image has 1 to 128 groups and one has exactly that many. `owners`: among the 256 merged tokens of one pack no owner gets more than 8; in some pack an owner gets exactly 8.
All inputs are finite; a program needn't handle non-finite values.
Results may differ from a plain program's by a relative error of at most 0.015.
Values may be sent and summed in bfloat16 or wider, within the bound.
No kernel may reach another device: no remote copies, remote signals or barrier semaphores. Data moves between devices by JAX's collectives and lax.ppermute only.
A program may use at most 64 MiB of HBM per device.

v0:
```python
import jax
import jax.numpy as jnp
from jax import lax
from jax.sharding import PartitionSpec as P


def layer_norm(values, gain, shift):
    wide = values.astype(jnp.float32)
    average = jnp.mean(wide, axis=-1, keepdims=True)
    centred = wide - average
    variance = jnp.mean(centred * centred, axis=-1, keepdims=True)
    return centred * lax.rsqrt(variance + 1e-06) * gain + shift


def attend(heads_qkv, token_segs):
    row_count = heads_qkv.shape[0]
    width = heads_qkv.shape[2] // 3
    queries = heads_qkv[:, :, :width]
    keys_all = heads_qkv[:, :, width : 2 * width]
    values_all = heads_qkv[:, :, 2 * width :]
    score_scale = 1.0 / jnp.sqrt(jnp.float32(width))
    block_rows = min(512, row_count)
    outputs = []
    for block_index in range(row_count // block_rows):
        lower = block_index * block_rows
        scores = (
            jnp.einsum(
                "qhd,khd->hqk",
                queries[lower : lower + block_rows],
                keys_all,
                preferred_element_type=jnp.float32,
            )
            * score_scale
        )
        same = token_segs[lower : lower + block_rows][:, None] == token_segs[None, :]
        scores = jnp.where(same[None], scores, -jnp.inf)
        row_max = jnp.max(scores, axis=-1, keepdims=True)
        exponent = jnp.exp(scores - row_max)
        probs = (exponent / jnp.sum(exponent, axis=-1, keepdims=True)).astype(jnp.bfloat16)
        context = jnp.einsum("hqk,khd->qhd", probs, values_all, preferred_element_type=jnp.float32)
        outputs.append(context.astype(jnp.bfloat16))
    return jnp.concatenate(outputs, axis=0)


def shards(
    tokens,
    ln1_gain,
    ln1_shift,
    w_qkv,
    w_out,
    ln2_gain,
    ln2_shift,
    w_proj,
    proj_bias,
    segments,
    owners,
):
    dp_count = lax.axis_size("dp")
    gathered = lax.all_gather(tokens, "tensor", axis=0, tiled=True)
    row_count = gathered.shape[0]
    normed = layer_norm(gathered, ln1_gain, ln1_shift).astype(jnp.bfloat16)
    heads_here = w_qkv.shape[1]
    heads_qkv = jnp.dot(
        normed, w_qkv.reshape(w_qkv.shape[0], -1), preferred_element_type=jnp.float32
    )
    heads_qkv = heads_qkv.astype(jnp.bfloat16).reshape(row_count, heads_here, -1)
    token_segs = jnp.repeat(segments[0], 4)
    context = attend(heads_qkv, token_segs).reshape(row_count, -1)
    out_flat = w_out.reshape(-1, w_out.shape[2])
    attn_all = lax.psum(
        jnp.dot(context, out_flat, preferred_element_type=jnp.float32).astype(jnp.bfloat16),
        "tensor",
    ).astype(jnp.float32)
    hidden = (gathered.astype(jnp.float32) + attn_all).astype(jnp.bfloat16)
    normed_all = layer_norm(hidden, ln2_gain, ln2_shift).astype(jnp.bfloat16)
    groups = row_count // 4
    merged = normed_all.reshape(groups, -1)
    summed = jnp.dot(
        merged, lax.all_gather(w_proj, "dp", axis=0, tiled=True), preferred_element_type=jnp.float32
    )
    projected = (summed + proj_bias).astype(jnp.bfloat16)
    dests = owners[:, 0]
    onehot = (dests[:, None] == jnp.arange(dp_count, dtype=jnp.int32)[None, :]).astype(jnp.int32)
    earlier = jnp.cumsum(onehot, axis=0) - onehot
    position = jnp.sum(earlier * onehot, axis=1)
    capacity = 2 * groups // dp_count
    slot_index = dests * capacity + position
    scatter_table = (
        slot_index[None, :] == jnp.arange(dp_count * capacity, dtype=jnp.int32)[:, None]
    ).astype(jnp.bfloat16)
    outgoing = jnp.dot(scatter_table, projected, preferred_element_type=jnp.float32).astype(
        jnp.bfloat16
    )
    outgoing = outgoing.reshape(dp_count, capacity, -1)
    arrived = lax.all_to_all(outgoing, "dp", split_axis=0, concat_axis=0, tiled=True)
    return arrived.reshape(dp_count * capacity, -1)


def solution(mesh):
    return jax.shard_map(
        shards,
        mesh=mesh,
        in_specs=(
            P(("dp", "tensor"), None),
            P(),
            P(),
            P(None, "tensor", None),
            P("tensor", None, None),
            P(),
            P(),
            P("dp", "tensor"),
            P("tensor"),
            P("dp", None),
            P("dp", None),
        ),
        out_specs=P("dp", "tensor"),
        check_vma=False,
    )
```

profile of v0, /device:TPU:8, one launch (start us, length us, event | category | flops | bytes accessed | tf_op | source)
XLA Modules:
  0.0 273.7 jit_solution(15908829058235544437)
XLA Ops:
  7.4 0.7 all-gather.3.cloned.1.call-update
  8.1 0.7 slice_bitcast_fusion.1
  9.2 0.8 broadcast_in_dim.25
  10.0 0.1 eq.86
  10.1 0.7 broadcast_compare_fusion.1
  10.8 38.3 %all-gather.3.cloned.1.call-done = bf16[1024,1408]{1,0:T(8,128)(2,1)} async-done(((bf16[128,1408]{1,0:T(8,128)(2,1)}), bf16[1024,1408]{1,0:T(8,128)(2,1)}) %all-gather.3.cloned.1.call-update) | async-done | bytes 2883600 | tf_op jit(solution)/shard_map/all_gather | solution.py:59
  49.1 2.4 convert_reduce_fusion
  51.5 0.3 copy-done.1
  51.7 0.9 fusion.6
  52.7 3.1 %fusion.31 = bf16[1024,528]{0,1:T(8,128)(2,1)} fusion(bf16[1408,528]{0,1:T(8,128)(2,1)S(1)} %bitcast.40, bf16[1024,1408]{1,0:T(8,128)(2,1)S(1)} %copy-done.1, f32[1408]{0:T(1024)S(1)} %copy-done.8, f32[1408]{0:T(1024)S(1)} %copy-done.9, f32[1024]{0:T(1024)S(1)} %add_rsqrt_fusion.1, f32[1024]{0:T(1024)S(1)} %broadcast_multiply_fusion.1), kind=kOutput, calls=%fused_computation.42 | convolution fusion | flops 1531723776 | bytes 5471232 | tf_op jit(solution)/shard_map/dot_general | solution.py:63
  55.8 4.8 %fusion.90 = (f32[2,512]{1,0:T(2,128)S(1)}, f32[2,512,1024]{2,1,0:T(8,128)}) fusion(pred[512,1024]{1,0:T(8,128)(4,1)S(1)} %get-tuple-element.5, bf16[1024,2,264]{0,2,1:T(8,128)(2,1)} %bitcast.47), kind=kOutput, calls=%fused_computation.94 | convolution fusion | flops 188744704 | bytes 5263360 | tf_op jit(solution)/shard_map/sub | solution.py:38
  60.6 4.9 %fusion.81 = (f32[2,512]{1,0:T(2,128)S(1)}, f32[2,512,1024]{2,1,0:T(8,128)}) fusion(pred[512,1024]{1,0:T(8,128)(4,1)S(1)} %get-tuple-element.6, bf16[1024,2,264]{0,2,1:T(8,128)(2,1)} %bitcast.48), kind=kOutput, calls=%fused_computation.93 | convolution fusion | flops 188744704 | bytes 5263360 | tf_op jit(solution)/shard_map/sub | solution.py:38
  65.4 3.2 %fusion.37 = bf16[512,2,88]{0,2,1:T(8,128)(2,1)S(1)} fusion(f32[2,512,1024]{2,1,0:T(8,128)} %get-tuple-element.12, f32[2,512]{1,0:T(2,128)S(1)} %get-tuple-element.11, bf16[1024,2,264]{0,2,1:T(8,128)(2,1)S(1)} %bitcast.49), kind=kOutput, calls=%fused_computation.48 | convolution fusion | flops 186736640 | bytes 4739072 | tf_op jit(solution)/shard_map/hqk,khd->qhd/dot_general | solution.py:40
  68.6 0.3 copy-done.12
  68.9 0.9 fusion.38
  69.7 0.2 copy-done.4
  69.9 2.7 bitcast_convert_fusion
  72.6 0.2 all-gather.5.cloned.1.call-start
  72.8 0.3 all-gather.5.cloned.1.call-update
  73.2 0.6 reduce-window.6
  73.8 0.2 slice_reduce_fusion
  74.2 83.9 %all-reduce.2.cloned.1.call-done = bf16[1024,1408]{1,0:T(8,128)(2,1)} async-done(((bf16[1024,1408]{1,0:T(8,128)(2,1)}), bf16[1024,1408]{1,0:T(8,128)(2,1)}) %all-reduce.2.cloned.1.call-update) | async-done | bytes 2883600 | tf_op jit(solution)/shard_map/psum | solution.py:70
  158.0 3.6 %convert_reduce_fusion.1 = f32[1024]{0:T(1024)S(1)} fusion(bf16[1024,1408]{1,0:T(8,128)(2,1)} %all-reduce.2.cloned.1.call-done, bf16[1024,1408]{1,0:T(8,128)(2,1)} %all-gather.3.cloned.1.call-done), kind=kLoop, calls=%fused_computation.6 | loop fusion | flops 8649728 | bytes 5771264 | tf_op jit(solution)/shard_map/reduce_sum | solution.py:9
  161.7 0.7 copy-done.3
  162.4 1.2 fusion.10
  163.7 2.9 %fusion.13 = bf16[1024,1408]{1,0:T(8,128)(2,1)} fusion(f32[1408]{0:T(1024)S(1)} %copy-done.6, f32[1408]{0:T(1024)S(1)} %copy-done.7, f32[1024]{0:T(1024)S(1)} %add_rsqrt_fusion, f32[1024]{0:T(1024)S(1)} %broadcast_multiply_fusion, bf16[1024,1408]{1,0:T(8,128)(2,1)S(1)} %copy-done.3, bf16[1024,1408]{1,0:T(8,128)(2,1)S(1)} %copy-done.2), kind=kLoop, calls=%fused_computation.18 | loop fusion | flops 14417920 | bytes 8670208 | tf_op jit(solution)/shard_map/convert_element_type | solution.py:75
  166.5 5.7 %reshape.149 = bf16[256,5632]{1,0:T(8,128)(2,1)} reshape(bf16[1024,1408]{1,0:T(8,128)(2,1)} %fusion.13) | data formatting | bytes 5767168 | tf_op jit(solution)/shard_map/reshape | solution.py:77
  172.2 54.6 %all-gather.5.cloned.1.call-done = bf16[5632,448]{1,0:T(8,128)(2,1)} async-done(((bf16[88,448]{1,0:T(8,128)(2,1)}), bf16[5632,448]{1,0:T(8,128)(2,1)}) %all-gather.5.cloned.1.call-update) | async-done | bytes 5046288 | tf_op jit(solution)/shard_map/all_gather | solution.py:79
  226.8 5.5 %convolution_convert_fusion = bf16[512,448]{0,1:T(8,128)(2,1)S(1)} fusion(bf16[256,5632]{1,0:T(8,128)(2,1)} %reshape.149, bf16[5632,448]{1,0:T(8,128)(2,1)} %all-gather.5.cloned.1.call-done, f32[448]{0:T(512)S(1)} %copy-done.10, s32[256]{0:T(256)S(1)} %multiply_add_fusion), kind=kOutput, calls=%fused_computation.43 | convolution fusion | flops 1409875968 | bytes 8391424 | tf_op jit(solution)/shard_map/dot_general | solution.py:91
  232.2 0.2 copy.13
  232.4 32.8 %all_to_all.5 = bf16[64,8,448]{2,1,0:T(8,128)(2,1)S(1)} all-to-all(bf16[64,8,448]{2,1,0:T(8,128)(2,1)S(1)} %bitcast.41), channel_id=1, replica_groups=mesh['dp'=64,'tensor'=8] {'dp'}, dimensions={0} | all-to-all | bytes 917504 | tf_op jit(solution)/shard_map/all_to_all | solution.py:95
  265.3 1.0 copy.14
  (38 shorter events, 0.7 us)
Async XLA Ops:
  7.4 45.3 %copy-start = (bf16[1408,2,264]{0,2,1:T(8,128)(2,1)S(1)}, bf16[1408,2,264]{0,2,1:T(8,128)(2,1)}, u32[]{:S(2)}) copy-start(bf16[1408,2,264]{0,2,1:T(8,128)(2,1)} %param.14) | copy-start | bytes 4460548
  7.4 45.3 %copy-start.9 = (f32[1408]{0:T(1024)S(1)}, f32[1408]{0:T(1024)}, u32[]{:S(2)}) copy-start(f32[1408]{0:T(1024)} %param.12) | copy-start | bytes 16900
  7.4 45.3 %copy-start.8 = (f32[1408]{0:T(1024)S(1)}, f32[1408]{0:T(1024)}, u32[]{:S(2)}) copy-start(f32[1408]{0:T(1024)} %param.13) | copy-start | bytes 16900
  7.4 41.7 %all-gather.3.cloned.1.call-start = ((), (), s32[]{:S(2)}) async-start(), calls=%async_computation.1 | async-start | bytes 3244032 | tf_op jit(solution)/shard_map/all_gather | solution.py:59
  8.1 149.9 %all-reduce.2.cloned.1.call-start = ((), (), s32[]{:S(2)}) async-start(), calls=%async_computation.2 | async-start | bytes 5767168 | tf_op jit(solution)/shard_map/psum | solution.py:70
  49.1 2.7 copy-start.1
  60.6 4.9 %copy-start.11 = (bf16[1024,528]{0,1:T(8,128)(2,1)S(1)}, bf16[1024,528]{0,1:T(8,128)(2,1)}, u32[]{:S(2)}) copy-start(bf16[1024,528]{0,1:T(8,128)(2,1)} %fusion.31) | copy-start | bytes 3244036
  65.4 3.4 %copy-start.12 = (f32[2,512,1024]{2,1,0:T(8,128)S(1)}, f32[2,512,1024]{2,1,0:T(8,128)}, u32[]{:S(2)}) copy-start(f32[2,512,1024]{2,1,0:T(8,128)} %get-tuple-element.10) | copy-start | bytes 12582916
  68.9 1.0 copy-start.4
  69.9 3.3 %copy-start.5 = (s32[256,1]{0,1:T(1,128)S(1)}, s32[256,1]{0,1:T(1,128)}, u32[]{:S(2)}) copy-start(s32[256,1]{0,1:T(1,128)} %param.21) | copy-start | bytes 3076
  72.6 154.1 %all-gather.5.cloned.1.call-start = ((), (), s32[]{:S(2)}) async-start(), calls=%async_computation.3 | async-start | bytes 5857280 | tf_op jit(solution)/shard_map/all_gather | solution.py:79
  158.0 3.7 %copy-start.2 = (bf16[1024,1408]{1,0:T(8,128)(2,1)S(1)}, bf16[1024,1408]{1,0:T(8,128)(2,1)}, u32[]{:S(2)}) copy-start(bf16[1024,1408]{1,0:T(8,128)(2,1)} %all-gather.3.cloned.1.call-done) | copy-start | bytes 8650756
  158.0 4.4 %copy-start.3 = (bf16[1024,1408]{1,0:T(8,128)(2,1)S(1)}, bf16[1024,1408]{1,0:T(8,128)(2,1)}, u32[]{:S(2)}) copy-start(bf16[1024,1408]{1,0:T(8,128)(2,1)} %all-reduce.2.cloned.1.call-done) | copy-start | bytes 8650756
  161.7 2.0 copy-start.6
  161.7 2.0 copy-start.7
  166.5 60.2 %copy-start.10 = (f32[448]{0:T(512)S(1)}, f32[448]{0:T(512)}, u32[]{:S(2)}) copy-start(f32[448]{0:T(512)} %param.19) | copy-start | bytes 5380
Sparse Core Ops, SparseCore 0:
  10.3 38.6 all-gather.2
  72.7 85.2 all-reduce.1
Sparse Core Ops, SparseCore 1:
  76.0 150.7 all-gather.4
where the time goes:
time: 274 us
  waiting for transfers between devices  178 us (65%)
  blocking collectives  32.8 us (12%)
  matrix products  24.9 us (9%)
  between operations  15 us (5%)
  other arithmetic  12.5 us (5%)
  local copies, waits for them, and re-layouts  10.4 us (4%)
    psum x1, waiting for transfers between devices, shards(): lax.psum(jnp.dot(context, out_flat, preferred_element_type=jnp.float32).a...  83.9 us
    all_gather x1, waiting for transfers between devices, shards(): lax.all_gather(w_proj, 'dp', axis=0, tiled=True)  54.6 us
    all_gather x1, waiting for transfers between devices, shards(): gathered = lax.all_gather(tokens, 'tensor', axis=0, tiled=True)  38.3 us
    all_to_all x1, blocking collectives, shards(): lax.all_to_all(outgoing, 'dp', split_axis=0, concat_axis=0, tiled=True)  32.8 us
    sub x2, matrix products, attend(): exponent = jnp.exp(scores - row_max)  9.63 us
    reduce_sum x2, other arithmetic, layer_norm(): average = jnp.mean(wide, axis=-1, keepdims=True)  6.05 us
    reshape x1, local copies, waits for them, and re-layouts, shards(): merged = normed_all.reshape(groups, -1)  5.67 us
  transfers between devices with their start and end apart: 3, of which 3 were waited for; matrix products, arithmetic and copies ran while one was open for 6% of the time, Pallas kernels for 0%

commit v1 on v0

--- a/solution.py
+++ b/solution.py
@@ -56,7 +56,14 @@
     owners,
 ):
     dp_count = lax.axis_size("dp")
-    gathered = lax.all_gather(tokens, "tensor", axis=0, tiled=True)
+    ring = [tokens]
+    for hop in range(7):
+        ring.append(lax.ppermute(ring[-1], "tensor", [(dev, (dev + 1) % 8) for dev in range(8)]))
+    gathered = jnp.roll(
+        jnp.concatenate(ring[::-1], axis=0),
+        (lax.axis_index("tensor") + 1) * ring[0].shape[0],
+        axis=0,
+    )
     row_count = gathered.shape[0]
     normed = layer_norm(gathered, ln1_gain, ln1_shift).astype(jnp.bfloat16)
     heads_here = w_qkv.shape[1]

time: 274 us -> 295 us (1.077)
  waiting for transfers between devices: 178 us -> 195 us
  local copies, waits for them, and re-layouts: 10.4 us -> 15.7 us
    ppermute x0 -> x7, waiting for transfers between devices: none -> 53.4 us  [shards(): lax.ppermute(ring[-1], 'tensor', [(dev, (dev + 1) % 8) for dev in range(8)])]
    all_gather x1 -> x0, waiting for transfers between devices: 38.3 us -> none  [shards(): gathered = lax.all_gather(tokens, 'tensor', axis=0, tiled=True)]
    unnamed x26 -> x47, local copies, waits for them, and re-layouts: 1.42 us -> 6.68 us
  transfers between devices with their start and end apart: 3 -> 9, of which waited for: 3 -> 9; matrix products, arithmetic and copies ran while one was open for 6% -> 6% of each run, Pallas kernels for 0% -> 0%
where the time goes in v1:
time: 295 us
  waiting for transfers between devices  195 us (66%)
  blocking collectives  32.9 us (11%)
  matrix products  24.9 us (8%)
  local copies, waits for them, and re-layouts  15.7 us (5%)
  between operations  15.2 us (5%)
  other arithmetic  11 us (4%)
    psum x1, waiting for transfers between devices, shards(): lax.psum(jnp.dot(context, out_flat, preferred_element_type=jnp.float32).a...  85.2 us
    all_gather x1, waiting for transfers between devices, shards(): lax.all_gather(w_proj, 'dp', axis=0, tiled=True)  55.8 us
    ppermute x7, waiting for transfers between devices, shards(): lax.ppermute(ring[-1], 'tensor', [(dev, (dev + 1) % 8) for dev in range(8)])  53.4 us
    all_to_all x1, blocking collectives, shards(): lax.all_to_all(outgoing, 'dp', split_axis=0, concat_axis=0, tiled=True)  32.9 us
    sub x2, matrix products, attend(): exponent = jnp.exp(scores - row_max)  9.67 us
    unnamed x47, local copies, waits for them, and re-layouts  6.68 us
  transfers between devices with their start and end apart: 9, of which 9 were waited for; matrix products, arithmetic and copies ran while one was open for 6% of the time, Pallas kernels for 0%

profile of v1, /device:TPU:8, one launch (start us, length us, event | category | flops | bytes accessed | tf_op | source)
XLA Modules:
  0.0 294.5 jit_solution(10161435184993514373)
XLA Ops:
  7.4 8.3 %collective-permute-done = bf16[128,1408]{1,0:T(8,128)(2,1)S(1)} collective-permute-done((bf16[128,1408]{1,0:T(8,128)(2,1)}, bf16[128,1408]{1,0:T(8,128)(2,1)S(1)}, u32[]{:S(2)}, u32[]{:S(2)}) %collective-permute-start) | collective-permute-done | bytes 360480 | tf_op jit(solution)/shard_map/ppermute | solution.py:61
  15.7 8.1 %collective-permute-done.1 = bf16[128,1408]{1,0:T(8,128)(2,1)S(1)} collective-permute-done((bf16[128,1408]{1,0:T(8,128)(2,1)S(1)}, bf16[128,1408]{1,0:T(8,128)(2,1)S(1)}, u32[]{:S(2)}, u32[]{:S(2)}) %collective-permute-start.1) | collective-permute-done | bytes 360480 | tf_op jit(solution)/shard_map/ppermute | solution.py:61
  23.7 8.1 %collective-permute-done.2 = bf16[128,1408]{1,0:T(8,128)(2,1)S(1)} collective-permute-done((bf16[128,1408]{1,0:T(8,128)(2,1)S(1)}, bf16[128,1408]{1,0:T(8,128)(2,1)S(1)}, u32[]{:S(2)}, u32[]{:S(2)}) %collective-permute-start.2) | collective-permute-done | bytes 360480 | tf_op jit(solution)/shard_map/ppermute | solution.py:61
  31.8 8.1 %collective-permute-done.3 = bf16[128,1408]{1,0:T(8,128)(2,1)S(1)} collective-permute-done((bf16[128,1408]{1,0:T(8,128)(2,1)S(1)}, bf16[128,1408]{1,0:T(8,128)(2,1)S(1)}, u32[]{:S(2)}, u32[]{:S(2)}) %collective-permute-start.3) | collective-permute-done | bytes 360480 | tf_op jit(solution)/shard_map/ppermute | solution.py:61
  39.8 8.1 %collective-permute-done.4 = bf16[128,1408]{1,0:T(8,128)(2,1)S(1)} collective-permute-done((bf16[128,1408]{1,0:T(8,128)(2,1)S(1)}, bf16[128,1408]{1,0:T(8,128)(2,1)S(1)}, u32[]{:S(2)}, u32[]{:S(2)}) %collective-permute-start.4) | collective-permute-done | bytes 360480 | tf_op jit(solution)/shard_map/ppermute | solution.py:61
  47.9 0.7 copy-done.3
  48.6 8.2 %collective-permute-done.5 = bf16[128,1408]{1,0:T(8,128)(2,1)} collective-permute-done((bf16[128,1408]{1,0:T(8,128)(2,1)S(1)}, bf16[128,1408]{1,0:T(8,128)(2,1)}, u32[]{:S(2)}, u32[]{:S(2)}) %collective-permute-start.5) | collective-permute-done | bytes 360480 | tf_op jit(solution)/shard_map/ppermute | solution.py:61
  56.8 0.7 slice_bitcast_fusion.1
  57.9 0.8 broadcast_in_dim.25
  58.8 1.7 broadcast_compare_fusion.1
  60.4 4.7 %collective-permute-done.6 = bf16[128,1408]{1,0:T(8,128)(2,1)} collective-permute-done((bf16[128,1408]{1,0:T(8,128)(2,1)}, bf16[128,1408]{1,0:T(8,128)(2,1)}, u32[]{:S(2)}, u32[]{:S(2)}) %collective-permute-start.6) | collective-permute-done | bytes 360480 | tf_op jit(solution)/shard_map/ppermute | solution.py:61
  65.2 1.0 constant_dynamic-update-slice_fusion.15
  66.2 1.0 constant_dynamic-update-slice_fusion.14
  67.2 1.0 constant_dynamic-update-slice_fusion.13
  68.5 1.0 constant_dynamic-update-slice_fusion.7
  69.5 1.0 constant_dynamic-update-slice_fusion.6
  71.3 0.9 fusion.6
  72.2 3.1 %fusion.32 = bf16[1024,528]{0,1:T(8,128)(2,1)} fusion(bf16[1408,528]{0,1:T(8,128)(2,1)S(1)} %bitcast.40, f32[1408]{0:T(1024)S(1)} %copy-done.11, f32[1408]{0:T(1024)S(1)} %copy-done.12, f32[1024]{0:T(1024)S(1)} %add_rsqrt_fusion.1, f32[1024]{0:T(1024)S(1)} %broadcast_multiply_fusion.1, bf16[2048,1408]{1,0:T(8,128)(2,1)S(1)} %constant_dynamic-update-slice_fusion, ...), kind=kOutput, calls=%fused_computation.43 | convolution fusion | flops 1531723776 | bytes 5476356 | tf_op jit(solution)/shard_map/dot_general | solution.py:70
  75.4 4.8 %fusion.93 = (f32[2,512]{1,0:T(2,128)S(1)}, f32[2,512,1024]{2,1,0:T(8,128)}) fusion(pred[512,1024]{1,0:T(8,128)(4,1)S(1)} %copy-done.6, bf16[1024,2,264]{0,2,1:T(8,128)(2,1)} %bitcast.47), kind=kOutput, calls=%fused_computation.112 | convolution fusion | flops 188744704 | bytes 5263360 | tf_op jit(solution)/shard_map/sub | solution.py:38
  80.1 4.9 %fusion.84 = (f32[2,512]{1,0:T(2,128)S(1)}, f32[2,512,1024]{2,1,0:T(8,128)}) fusion(pred[512,1024]{1,0:T(8,128)(4,1)S(1)} %copy-done.5, bf16[1024,2,264]{0,2,1:T(8,128)(2,1)} %bitcast.48), kind=kOutput, calls=%fused_computation.111 | convolution fusion | flops 188744704 | bytes 5263360 | tf_op jit(solution)/shard_map/sub | solution.py:38
  85.0 3.2 %fusion.38 = bf16[512,2,88]{0,2,1:T(8,128)(2,1)S(1)} fusion(f32[2,512,1024]{2,1,0:T(8,128)} %get-tuple-element.14, f32[2,512]{1,0:T(2,128)S(1)} %get-tuple-element.13, bf16[1024,2,264]{0,2,1:T(8,128)(2,1)S(1)} %bitcast.49), kind=kOutput, calls=%fused_computation.49 | convolution fusion | flops 186736640 | bytes 4739072 | tf_op jit(solution)/shard_map/hqk,khd->qhd/dot_general | solution.py:40
  88.5 0.9 fusion.39
  89.5 2.6 bitcast_convert_fusion
  93.7 85.2 %all-reduce.2.cloned.1.call-done = bf16[1024,1408]{1,0:T(8,128)(2,1)} async-done(((bf16[1024,1408]{1,0:T(8,128)(2,1)}), bf16[1024,1408]{1,0:T(8,128)(2,1)}) %all-reduce.2.cloned.1.call-update) | async-done | bytes 2883600 | tf_op jit(solution)/shard_map/psum | solution.py:77
  178.9 3.6 %convert_reduce_fusion.1 = (f32[1024]{0:T(1024)S(1)}, bf16[1024,1408]{1,0:T(8,128)(2,1)S(1)}) fusion(bf16[1024,1408]{1,0:T(8,128)(2,1)} %all-reduce.2.cloned.1.call-done, bf16[2048,1408]{1,0:T(8,128)(2,1)} %copy-done.1, s32[]{:T(128)S(6)} %select_n.21), kind=kLoop, calls=%fused_computation.6 | loop fusion | flops 8649728 | bytes 8654852 | tf_op jit(solution)/shard_map/reduce_sum | solution.py:9
  182.5 0.9 fusion.10
  183.4 2.7 fusion.13
  186.1 5.6 %reshape.149 = bf16[256,5632]{1,0:T(8,128)(2,1)} reshape(bf16[1024,1408]{1,0:T(8,128)(2,1)} %fusion.13) | data formatting | bytes 5767168 | tf_op jit(solution)/shard_map/reshape | solution.py:84
  191.8 55.8 %all-gather.2.cloned.1.call-done = bf16[5632,448]{1,0:T(8,128)(2,1)} async-done(((bf16[88,448]{1,0:T(8,128)(2,1)}), bf16[5632,448]{1,0:T(8,128)(2,1)}) %all-gather.2.cloned.1.call-update) | async-done | bytes 5046288 | tf_op jit(solution)/shard_map/all_gather | solution.py:86
  247.6 5.5 %convolution_convert_fusion = bf16[512,448]{0,1:T(8,128)(2,1)S(1)} fusion(bf16[256,5632]{1,0:T(8,128)(2,1)} %reshape.149, bf16[5632,448]{1,0:T(8,128)(2,1)} %all-gather.2.cloned.1.call-done, f32[448]{0:T(512)S(1)} %copy-done.13, s32[256]{0:T(256)S(1)} %multiply_add_fusion), kind=kOutput, calls=%fused_computation.44 | convolution fusion | flops 1409875968 | bytes 8391424 | tf_op jit(solution)/shard_map/dot_general | solution.py:98
  253.2 32.9 %all_to_all.5 = bf16[64,8,448]{2,1,0:T(8,128)(2,1)S(1)} all-to-all(bf16[64,8,448]{2,1,0:T(8,128)(2,1)S(1)} %bitcast.41), channel_id=1, replica_groups=mesh['dp'=64,'tensor'=8] {'dp'}, dimensions={0} | all-to-all | bytes 917504 | tf_op jit(solution)/shard_map/all_to_all | solution.py:102
  286.1 1.0 copy.14
  (71 shorter events, 3.6 us)
Async XLA Ops:
  7.4 64.8 %copy-start = (bf16[1408,2,264]{0,2,1:T(8,128)(2,1)S(1)}, bf16[1408,2,264]{0,2,1:T(8,128)(2,1)}, u32[]{:S(2)}) copy-start(bf16[1408,2,264]{0,2,1:T(8,128)(2,1)} %param.14) | copy-start | bytes 4460548
  7.4 61.0 %copy-start.2 = (bf16[128,1408]{1,0:T(8,128)(2,1)S(1)}, bf16[128,1408]{1,0:T(8,128)(2,1)}, u32[]{:S(2)}) copy-start(bf16[128,1408]{1,0:T(8,128)(2,1)} %param.11) | copy-start | bytes 1081348
  7.4 171.5 %all-reduce.2.cloned.1.call-start = ((), (), s32[]{:S(2)}) async-start(), calls=%async_computation.1 | async-start | bytes 5767168 | tf_op jit(solution)/shard_map/psum | solution.py:77
  7.4 8.3 %collective-permute-start = (bf16[128,1408]{1,0:T(8,128)(2,1)}, bf16[128,1408]{1,0:T(8,128)(2,1)S(1)}, u32[]{:S(2)}, u32[]{:S(2)}) collective-permute-start(bf16[128,1408]{1,0:T(8,128)(2,1)} %param.11), channel_id=1, source_target_pairs={{0,1},{1,2},{2,3},{3,4},{4,5},{5,6},{6,7},{7,0},{8,9},{9,10},{10,1... | collective-permute-start | bytes 1081352 | tf_op jit(solution)/shard_map/ppermute | solution.py:61
  15.6 8.1 %collective-permute-start.1 = (bf16[128,1408]{1,0:T(8,128)(2,1)S(1)}, bf16[128,1408]{1,0:T(8,128)(2,1)S(1)}, u32[]{:S(2)}, u32[]{:S(2)}) collective-permute-start(bf16[128,1408]{1,0:T(8,128)(2,1)S(1)} %collective-permute-done), channel_id=1, source_target_pairs={{0,1},{1,2},{2,3},{3,4},{4,5},{5,6},{6,7},{7,0},{8,9},{9,10},{10,1... | collective-permute-start | bytes 1081352 | tf_op jit(solution)/shard_map/ppermute | solution.py:61
  23.7 8.1 %collective-permute-start.2 = (bf16[128,1408]{1,0:T(8,128)(2,1)S(1)}, bf16[128,1408]{1,0:T(8,128)(2,1)S(1)}, u32[]{:S(2)}, u32[]{:S(2)}) collective-permute-start(bf16[128,1408]{1,0:T(8,128)(2,1)S(1)} %collective-permute-done.1), channel_id=1, source_target_pairs={{0,1},{1,2},{2,3},{3,4},{4,5},{5,6},{6,7},{7,0},{8,9},{9,10},{10,1... | collective-permute-start | bytes 1081352 | tf_op jit(solution)/shard_map/ppermute | solution.py:61
  31.8 8.1 %collective-permute-start.3 = (bf16[128,1408]{1,0:T(8,128)(2,1)S(1)}, bf16[128,1408]{1,0:T(8,128)(2,1)S(1)}, u32[]{:S(2)}, u32[]{:S(2)}) collective-permute-start(bf16[128,1408]{1,0:T(8,128)(2,1)S(1)} %collective-permute-done.2), channel_id=1, source_target_pairs={{0,1},{1,2},{2,3},{3,4},{4,5},{5,6},{6,7},{7,0},{8,9},{9,10},{10,1... | collective-permute-start | bytes 1081352 | tf_op jit(solution)/shard_map/ppermute | solution.py:61
  39.8 8.1 %collective-permute-start.4 = (bf16[128,1408]{1,0:T(8,128)(2,1)S(1)}, bf16[128,1408]{1,0:T(8,128)(2,1)S(1)}, u32[]{:S(2)}, u32[]{:S(2)}) collective-permute-start(bf16[128,1408]{1,0:T(8,128)(2,1)S(1)} %collective-permute-done.3), channel_id=1, source_target_pairs={{0,1},{1,2},{2,3},{3,4},{4,5},{5,6},{6,7},{7,0},{8,9},{9,10},{10,1... | collective-permute-start | bytes 1081352 | tf_op jit(solution)/shard_map/ppermute | solution.py:61
  47.9 0.7 copy-start.3
  48.6 8.2 %collective-permute-start.5 = (bf16[128,1408]{1,0:T(8,128)(2,1)S(1)}, bf16[128,1408]{1,0:T(8,128)(2,1)}, u32[]{:S(2)}, u32[]{:S(2)}) collective-permute-start(bf16[128,1408]{1,0:T(8,128)(2,1)S(1)} %collective-permute-done.4), channel_id=1, source_target_pairs={{0,1},{1,2},{2,3},{3,4},{4,5},{5,6},{6,7},{7,0},{8,9},{9,10},{10,1... | collective-permute-start | bytes 1081352 | tf_op jit(solution)/shard_map/ppermute | solution.py:61
  56.8 8.4 %collective-permute-start.6 = (bf16[128,1408]{1,0:T(8,128)(2,1)}, bf16[128,1408]{1,0:T(8,128)(2,1)}, u32[]{:S(2)}, u32[]{:S(2)}) collective-permute-start(bf16[128,1408]{1,0:T(8,128)(2,1)} %collective-permute-done.5), channel_id=1, source_target_pairs={{0,1},{1,2},{2,3},{3,4},{4,5},{5,6},{6,7},{7,0},{8,9},{9,10},{10,1... | collective-permute-start | bytes 1081352 | tf_op jit(solution)/shard_map/ppermute | solution.py:61
  58.8 11.8 %copy-start.4 = (bf16[128,1408]{1,0:T(8,128)(2,1)S(1)}, bf16[128,1408]{1,0:T(8,128)(2,1)}, u32[]{:S(2)}) copy-start(bf16[128,1408]{1,0:T(8,128)(2,1)} %copy-done.3) | copy-start | bytes 1081348
  68.5 3.7 %copy-start.11 = (f32[1408]{0:T(1024)S(1)}, f32[1408]{0:T(1024)}, u32[]{:S(2)}) copy-start(f32[1408]{0:T(1024)} %param.13) | copy-start | bytes 16900
  68.5 3.7 %copy-start.12 = (f32[1408]{0:T(1024)S(1)}, f32[1408]{0:T(1024)}, u32[]{:S(2)}) copy-start(f32[1408]{0:T(1024)} %param.12) | copy-start | bytes 16900
  70.8 4.5 %copy-start.1 = (bf16[2048,1408]{1,0:T(8,128)(2,1)}, bf16[2048,1408]{1,0:T(8,128)(2,1)S(1)}, u32[]{:S(2)}) copy-start(bf16[2048,1408]{1,0:T(8,128)(2,1)S(1)} %constant_dynamic-update-slice_fusion) | copy-start | bytes 17301508
  72.2 3.1 %copy-start.6 = (pred[512,1024]{1,0:T(8,128)(4,1)S(1)}, pred[512,1024]{1,0:T(8,128)(4,1)}, u32[]{:S(2)}) copy-start(pred[512,1024]{1,0:T(8,128)(4,1)} %get-tuple-element.7) | copy-start | bytes 1572868
  75.3 4.8 %copy-start.5 = (pred[512,1024]{1,0:T(8,128)(4,1)S(1)}, pred[512,1024]{1,0:T(8,128)(4,1)}, u32[]{:S(2)}) copy-start(pred[512,1024]{1,0:T(8,128)(4,1)} %get-tuple-element.8) | copy-start | bytes 1572868
  80.1 4.9 %copy-start.14 = (bf16[1024,528]{0,1:T(8,128)(2,1)S(1)}, bf16[1024,528]{0,1:T(8,128)(2,1)}, u32[]{:S(2)}) copy-start(bf16[1024,528]{0,1:T(8,128)(2,1)} %fusion.32) | copy-start | bytes 3244036
  85.0 3.4 %copy-start.15 = (f32[2,512,1024]{2,1,0:T(8,128)S(1)}, f32[2,512,1024]{2,1,0:T(8,128)}, u32[]{:S(2)}) copy-start(f32[2,512,1024]{2,1,0:T(8,128)} %get-tuple-element.12) | copy-start | bytes 12582916
  88.5 1.0 copy-start.7
  89.5 3.2 %copy-start.8 = (s32[256,1]{0,1:T(1,128)S(1)}, s32[256,1]{0,1:T(1,128)}, u32[]{:S(2)}) copy-start(s32[256,1]{0,1:T(1,128)} %param.21) | copy-start | bytes 3076
  92.1 155.5 %all-gather.2.cloned.1.call-start = ((), (), s32[]{:S(2)}) async-start(), calls=%async_computation.2 | async-start | bytes 5857280 | tf_op jit(solution)/shard_map/all_gather | solution.py:86
  93.7 89.7 %copy-start.9 = (f32[1408]{0:T(1024)S(1)}, f32[1408]{0:T(1024)}, u32[]{:S(2)}) copy-start(f32[1408]{0:T(1024)} %param.17) | copy-start | bytes 16900
  93.7 89.7 %copy-start.10 = (f32[1408]{0:T(1024)S(1)}, f32[1408]{0:T(1024)}, u32[]{:S(2)}) copy-start(f32[1408]{0:T(1024)} %param.16) | copy-start | bytes 16900
  183.4 64.2 %copy-start.13 = (f32[448]{0:T(512)S(1)}, f32[448]{0:T(512)}, u32[]{:S(2)}) copy-start(f32[448]{0:T(512)} %param.19) | copy-start | bytes 5380
Sparse Core Ops, SparseCore 0:
  92.2 86.5 all-reduce.1
Sparse Core Ops, SparseCore 1:
  95.5 152.0 all-gather.1
